TPU v7x, 256 devices: a whole 4x4x8 slice. The times are simulated.
256 devices in a mesh: dp: 4 (over x), expert: 64 (over z, y, core).
Axes of the slice: x: 4, y: 4, z: 8, core: 2. Of those that a mesh axis runs over, the one named last changes fastest.
Arguments:
- tokens: bfloat16 [32768, 4096], P(('dp', 'expert')), may hold values from -6 to 6
- out_grad: bfloat16 [32768, 4096], P(('dp', 'expert')), may hold values from -0.75 to 0.75
- routes: int32 [32768, 1], P(('dp', 'expert')), may hold values from 0 to 63; in each aligned block of 128 rows (0 to 127, 128 to 255, ...) at most 3 rows name the same one
- gate_probs: bfloat16 [32768, 1], P(('dp', 'expert')), may hold values from 0.049804688 to 1
- w_gate: bfloat16 [64, 4096, 768], P('expert', None, 'dp'), may hold values from -0.09375 to 0.09375
- w_up: bfloat16 [64, 4096, 768], P('expert', None, 'dp'), may hold values from -0.09375 to 0.09375
- w_down: bfloat16 [64, 768, 4096], P('expert', 'dp'), may hold values from -0.21875 to 0.21875
Outputs:
- grad_tokens: bfloat16 [32768, 4096], P(('dp', 'expert'))
- grad_probs: bfloat16 [32768, 1], P(('dp', 'expert'))
- grad_w_gate: bfloat16 [64, 4096, 768], P('expert', None, 'dp')
- grad_w_up: bfloat16 [64, 4096, 768], P('expert', None, 'dp')
- grad_w_down: bfloat16 [64, 768, 4096], P('expert', 'dp')
Inputs may be any that keep to these rules, and one draw needn't show every extreme that they name: `routes`: the experts of one token are different. Among the 128 tokens of one device no expert is named more than 3 times, a bound that some block reaches.
All inputs are finite; a program needn't handle non-finite values.
Results may differ from a plain program's by a relative error of at most 0.018.
Values may be sent and summed in bfloat16 or wider, within the bound.
No kernel may reach another device: no remote copies, remote signals or barrier semaphores. Data moves between devices by JAX's collectives and lax.ppermute only.
A program may use at most 128 MiB of HBM per device.

v0:
```python
import jax
import jax.numpy as jnp
from jax import lax
from jax.sharding import PartitionSpec as P

LANES = 128
CHUNKS = 2


def body(tokens, out_grad, routes, gate_probs, w_gate, w_up, w_down):
    expert_count = lax.axis_size("expert")
    tok_count, width = tokens.shape
    top_count = routes.shape[1]
    capacity = 3 * tok_count * top_count // (2 * expert_count)
    slot_total = expert_count * capacity
    piece = width // CHUNKS
    per_peer = capacity * piece // LANES
    flat_routes = routes.reshape(-1)
    one_hot = (flat_routes[:, None] == jnp.arange(expert_count, dtype=jnp.int32)[None, :]).astype(
        jnp.int32
    )
    earlier = jnp.cumsum(one_hot, axis=0) - one_hot
    slot_index = jnp.sum(earlier * one_hot, axis=1)
    destination = flat_routes * capacity + slot_index
    placing = (jnp.arange(slot_total, dtype=jnp.int32)[:, None] == destination[None, :]).astype(
        jnp.bfloat16
    )
    collect = jnp.sum(placing.reshape(slot_total, tok_count, top_count), axis=2)
    contract_last = (((1,), (1,)), ((), ()))
    contract_first = (((0,), (0,)), ((), ()))

    def to_expert(rows):
        shaped = rows.reshape(expert_count, per_peer, LANES)
        return lax.all_to_all(shaped, "expert", 0, 0, tiled=True).reshape(slot_total, piece)

    def dispatch(source, c):
        part = source[:, c * piece : (c + 1) * piece]
        rows = jnp.dot(collect, part, preferred_element_type=jnp.float32).astype(jnp.bfloat16)
        return to_expert(rows)

    sent_prob = (
        jnp.dot(placing, gate_probs.reshape(-1), preferred_element_type=jnp.float32)
        .astype(jnp.bfloat16)
        .reshape(expert_count, capacity)
    )
    recv_prob = lax.all_to_all(sent_prob, "expert", 0, 0, tiled=True).reshape(slot_total)
    rows_in = []
    for c in range(CHUNKS):
        rows_in.append(lax.all_gather(dispatch(tokens, c), "dp", axis=0, tiled=True))
    rows_dy = []
    rows_prob = None
    for c in range(CHUNKS):
        recv = dispatch(out_grad, c)
        if c == 0:
            recv = jnp.concatenate(
                [recv, jnp.broadcast_to(recv_prob[:, None], (slot_total, LANES))], axis=1
            )
        gathered = lax.all_gather(recv, "dp", axis=0, tiled=True)
        if c == 0:
            rows_prob = gathered[:, piece]
            gathered = gathered[:, :piece]
        rows_dy.append(gathered)
    gate_w = w_gate[0]
    up_w = w_up[0]
    down_w = w_down[0]
    gate_pre = None
    up_pre = None
    for c in range(CHUNKS):
        g = jnp.dot(
            rows_in[c], gate_w[c * piece : (c + 1) * piece], preferred_element_type=jnp.float32
        )
        u = jnp.dot(
            rows_in[c], up_w[c * piece : (c + 1) * piece], preferred_element_type=jnp.float32
        )
        gate_pre = g if gate_pre is None else gate_pre + g
        up_pre = u if up_pre is None else up_pre + u
    sigmoid_gate = jax.nn.sigmoid(gate_pre)
    active = gate_pre * sigmoid_gate
    hidden = (active * up_pre).astype(jnp.bfloat16)
    back_raw = None
    for c in range(CHUNKS):
        b = lax.dot_general(
            rows_dy[c],
            down_w[:, c * piece : (c + 1) * piece],
            contract_last,
            preferred_element_type=jnp.float32,
        )
        back_raw = b if back_raw is None else back_raw + b
    score_part = jnp.sum(back_raw * hidden.astype(jnp.float32), axis=1)
    weight_col = rows_prob.astype(jnp.float32)[:, None]
    back_hidden = weight_col * back_raw
    grad_gate_pre = (
        back_hidden * up_pre * sigmoid_gate * (1.0 + gate_pre * (1.0 - sigmoid_gate))
    ).astype(jnp.bfloat16)
    grad_up_pre = (back_hidden * active).astype(jnp.bfloat16)
    row_total = grad_gate_pre.shape[0]
    back_rows = []
    back_scores = None
    for c in range(CHUNKS):
        part = lax.dot_general(
            grad_gate_pre,
            gate_w[c * piece : (c + 1) * piece],
            contract_last,
            preferred_element_type=jnp.float32,
        )
        part = part + lax.dot_general(
            grad_up_pre,
            up_w[c * piece : (c + 1) * piece],
            contract_last,
            preferred_element_type=jnp.float32,
        )
        if c == 0:
            part = jnp.concatenate(
                [part, jnp.broadcast_to(score_part[:, None], (row_total, LANES))], axis=1
            )
        own = lax.psum_scatter(part.astype(jnp.bfloat16), "dp", scatter_dimension=0, tiled=True)
        if c == 0:
            own_scores = own[:, piece].reshape(expert_count, capacity)
            back_scores = lax.all_to_all(own_scores, "expert", 0, 0, tiled=True).reshape(slot_total)
            own = own[:, :piece]
        back_rows.append(to_expert(own))
    grad_down = []
    grad_gate = []
    grad_up = []
    for c in range(CHUNKS):
        dy_c = rows_dy[c]
        scaled = (weight_col * dy_c.astype(jnp.float32)).astype(jnp.bfloat16)
        grad_down.append(
            lax.dot_general(
                hidden, scaled, contract_first, preferred_element_type=jnp.float32
            ).astype(jnp.bfloat16)
        )
        grad_gate.append(
            lax.dot_general(
                rows_in[c], grad_gate_pre, contract_first, preferred_element_type=jnp.float32
            ).astype(jnp.bfloat16)
        )
        grad_up.append(
            lax.dot_general(
                rows_in[c], grad_up_pre, contract_first, preferred_element_type=jnp.float32
            ).astype(jnp.bfloat16)
        )
    grad_down = jnp.concatenate(grad_down, axis=1)
    grad_gate = jnp.concatenate(grad_gate, axis=0)
    grad_up = jnp.concatenate(grad_up, axis=0)
    grad_tokens = jnp.concatenate(
        [
            lax.dot_general(
                collect, back_rows[c], contract_first, preferred_element_type=jnp.float32
            ).astype(jnp.bfloat16)
            for c in range(CHUNKS)
        ],
        axis=1,
    )
    grad_probs = (
        jnp.dot(back_scores, placing, preferred_element_type=jnp.float32)
        .astype(jnp.bfloat16)
        .reshape(tok_count, top_count)
    )
    return (grad_tokens, grad_probs, grad_gate[None], grad_up[None], grad_down[None])


def solution(mesh):
    in_specs = (
        P(("dp", "expert"), None),
        P(("dp", "expert"), None),
        P(("dp", "expert"), None),
        P(("dp", "expert"), None),
        P("expert", None, "dp"),
        P("expert", None, "dp"),
        P("expert", "dp", None),
    )
    out_specs = (
        P(("dp", "expert"), None),
        P(("dp", "expert"), None),
        P("expert", None, "dp"),
        P("expert", None, "dp"),
        P("expert", "dp", None),
    )
    return jax.shard_map(body, mesh=mesh, in_specs=in_specs, out_specs=out_specs, check_vma=False)
```

profile of v0, /device:TPU:1, one launch (start us, length us, event | category | flops | bytes accessed | tf_op | source)
XLA Modules:
  0.0 393.0 jit_solution(721865889223023181)
XLA Ops:
  11.5 35.9 %all_to_all.50 = bf16[64,48,128]{2,1,0:T(8,128)(2,1)S(1)} all-to-all(bf16[64,48,128]{2,1,0:T(8,128)(2,1)S(1)} %reshape.110), channel_id=1, replica_groups=mesh['dp'=4,'expert'=64] {'expert'}, dimensions={0} | all-to-all | bytes 1572864 | tf_op jit(solution)/shard_map/all_to_all | solution.py:34
  49.5 28.7 %all_to_all.51 = bf16[64,48,128]{2,1,0:T(8,128)(2,1)S(1)} all-to-all(bf16[64,48,128]{2,1,0:T(8,128)(2,1)S(1)} %reshape.112), channel_id=1, replica_groups=mesh['dp'=4,'expert'=64] {'expert'}, dimensions={0} | all-to-all | bytes 1572864 | tf_op jit(solution)/shard_map/all_to_all | solution.py:34
  80.4 5.9 %all-to-all-start.1 = ((bf16[64,1,3]{2,1,0:T(2,128)(2,1)}), bf16[64,1,3]{2,1,0:T(2,128)(2,1)S(1)}, u32[]{:S(2)}, u32[]{:S(2)}) async-start(bf16[64,1,3]{2,1,0:T(2,128)(2,1)} %all_to_all.40), calls=%async_computation.1 | async-start | bytes 65536 | tf_op jit(solution)/shard_map/all_to_all | solution.py:46
  87.9 7.7 %all-to-all-done.1 = bf16[64,1,3]{2,1,0:T(2,128)(2,1)S(1)} async-done(((bf16[64,1,3]{2,1,0:T(2,128)(2,1)}), bf16[64,1,3]{2,1,0:T(2,128)(2,1)S(1)}, u32[]{:S(2)}, u32[]{:S(2)}) %all-to-all-start.1) | async-done | bytes 416 | tf_op jit(solution)/shard_map/all_to_all | solution.py:46
  95.7 4.8 %all-to-all-start = ((bf16[64,48,128]{2,1,0:T(8,128)(2,1)}), bf16[64,48,128]{2,1,0:T(8,128)(2,1)S(1)}, u32[]{:S(2)}, u32[]{:S(2)}) async-start(bf16[64,48,128]{2,1,0:T(8,128)(2,1)} %reshape.105), calls=%async_computation | async-start | bytes 1572864 | tf_op jit(solution)/shard_map/all_to_all | solution.py:34
  100.7 22.9 %all-to-all-done = bf16[64,48,128]{2,1,0:T(8,128)(2,1)S(1)} async-done(((bf16[64,48,128]{2,1,0:T(8,128)(2,1)}), bf16[64,48,128]{2,1,0:T(8,128)(2,1)S(1)}, u32[]{:S(2)}, u32[]{:S(2)}) %all-to-all-start) | async-done | bytes 786464 | tf_op jit(solution)/shard_map/all_to_all | solution.py:34
  127.0 28.6 %all_to_all.52 = bf16[64,48,128]{2,1,0:T(8,128)(2,1)S(1)} all-to-all(bf16[64,48,128]{2,1,0:T(8,128)(2,1)S(1)} %reshape.108), channel_id=1, replica_groups=mesh['dp'=4,'expert'=64] {'expert'}, dimensions={0} | all-to-all | bytes 1572864 | tf_op jit(solution)/shard_map/all_to_all | solution.py:34
  157.1 4.1 %fusion.18 = f32[768,192]{0,1:T(8,128)} fusion(bf16[768,2048]{1,0:T(8,128)(2,1)} %all-gather.9.cloned.1.call-done, bf16[1,4096,192]{1,2,0:T(8,128)(2,1)S(1)} %copy-done.12), kind=kOutput, calls=%fused_computation.42 | convolution fusion | flops 603979776 | bytes 4521984 | tf_op jit(solution)/shard_map/dot_general | solution.py:69
  161.2 2.1 fusion.23
  163.3 4.4 %convolution_add_fusion = f32[768,192]{0,1:T(8,128)} fusion(f32[768,192]{0,1:T(8,128)} %fusion.18, bf16[768,2048]{1,0:T(8,128)(2,1)} %all-gather.11.cloned.1.call-done, bf16[1,4096,192]{1,2,0:T(8,128)(2,1)} %param.11), kind=kOutput, calls=%fused_computation.27 | convolution fusion | flops 604127232 | bytes 5111808 | tf_op jit(solution)/shard_map/dot_general | solution.py:69
  167.7 2.0 convolution_add_fusion.1
  169.7 8.5 %all-gather.5.cloned.1.call-done = bf16[768,2176]{1,0:T(8,128)(2,1)} async-done(((bf16[192,2176]{1,0:T(8,128)(2,1)}), bf16[768,2176]{1,0:T(8,128)(2,1)}) %all-gather.5.cloned.1.call-update) | async-done | bytes 3342352 | tf_op jit(solution)/shard_map/all_gather | solution.py:58
  179.3 4.1 %fusion.5 = f32[768,192]{0,1:T(8,128)} fusion(bf16[768,2176]{1,0:T(8,128)(2,1)} %all-gather.5.cloned.1.call-done, bf16[192,4096]{1,0:T(8,128)(2,1)} %bitcast.64), kind=kOutput, calls=%fused_computation.10 | convolution fusion | flops 603979776 | bytes 4521984 | tf_op jit(solution)/shard_map/dot_general | solution.py:82
  183.4 39.4 %all-gather.7.cloned.1.call-done = bf16[768,2048]{1,0:T(8,128)(2,1)} async-done(((bf16[192,2048]{1,0:T(8,128)(2,1)}), bf16[768,2048]{1,0:T(8,128)(2,1)}) %all-gather.7.cloned.1.call-update) | async-done | bytes 3145744 | tf_op jit(solution)/shard_map/all_gather | solution.py:58
  222.7 4.8 %multiply_reduce_fusion = (bf16[768]{0:T(1024)(128)(2,1)S(1)}, bf16[768,192]{0,1:T(8,128)(2,1)}, bf16[768,192]{0,1:T(8,128)(2,1)S(1)}, bf16[768,192]{0,1:T(8,128)(2,1)S(1)}) fusion(f32[768,192]{0,1:T(8,128)} %convolution_add_fusion.1, f32[768,192]{0,1:T(8,128)} %convolution_add_fusion, f32[768]{0:T(1024)S(1)} %convert_reduce_fusion, f32[768,192]{0,1:T(8,128)} %fusion.5, ...), kind=kOutput, calls=%fused_computation.57 | convolution fusion | flops 606928128 | bytes 6590976 | tf_op jit(solution)/shard_map/dot_general | solution.py:82
  230.3 2.0 pad_maximum_fusion
  232.4 2.3 fusion.13
  234.7 2.7 add_convert_fusion
  237.4 37.8 %reduce-scatter.3.cloned.1.call-done = bf16[192,2176]{1,0:T(8,128)(2,1)} async-done(((bf16[768,2176]{1,0:T(8,128)(2,1)}), bf16[192,2176]{1,0:T(8,128)(2,1)}) %reduce-scatter.3.cloned.1.call-update) | async-done | bytes 835600 | tf_op jit(solution)/shard_map/reduce_scatter | solution.py:116
  276.9 10.8 %all-to-all-start.7 = ((bf16[64,1,3]{2,1,0:T(2,128)(2,1)}), bf16[64,1,3]{2,1,0:T(2,128)(2,1)S(1)}, u32[]{:S(2)}, u32[]{:S(2)}) async-start(bf16[64,1,3]{2,1,0:T(2,128)(2,1)} %all_to_all.41), calls=%async_computation.9 | async-start | bytes 65536 | tf_op jit(solution)/shard_map/all_to_all | solution.py:119
  287.7 30.6 %reduce-scatter.5.cloned.1.call-done = bf16[192,2048]{1,0:T(8,128)(2,1)} async-done(((bf16[768,2048]{1,0:T(8,128)(2,1)}), bf16[192,2048]{1,0:T(8,128)(2,1)}) %reduce-scatter.5.cloned.1.call-update) | async-done | bytes 786448 | tf_op jit(solution)/shard_map/reduce_scatter | solution.py:116
  318.3 2.2 reshape.116
  320.4 10.9 %all-to-all-start.6 = ((bf16[64,48,128]{2,1,0:T(8,128)(2,1)}), bf16[64,48,128]{2,1,0:T(8,128)(2,1)}, u32[]{:S(2)}, u32[]{:S(2)}) async-start(bf16[64,48,128]{2,1,0:T(8,128)(2,1)} %reshape.116), calls=%async_computation.8 | async-start | bytes 1572864 | tf_op jit(solution)/shard_map/all_to_all | solution.py:34
  331.4 3.7 convolution_convert_fusion.3
  335.1 1.7 convolution_convert_fusion.1
  339.0 1.8 fusion.8
  340.8 1.8 fusion.7
  343.6 2.2 reshape.114
  345.8 8.5 %all-to-all-done.6 = bf16[64,48,128]{2,1,0:T(8,128)(2,1)} async-done(((bf16[64,48,128]{2,1,0:T(8,128)(2,1)}), bf16[64,48,128]{2,1,0:T(8,128)(2,1)}, u32[]{:S(2)}, u32[]{:S(2)}) %all-to-all-start.6) | async-done | bytes 786464 | tf_op jit(solution)/shard_map/all_to_all | solution.py:34
  354.3 6.1 %all-to-all-start.5 = ((bf16[64,48,128]{2,1,0:T(8,128)(2,1)}), bf16[64,48,128]{2,1,0:T(8,128)(2,1)}, u32[]{:S(2)}, u32[]{:S(2)}) async-start(bf16[64,48,128]{2,1,0:T(8,128)(2,1)} %reshape.114), calls=%async_computation.6 | async-start | bytes 1572864 | tf_op jit(solution)/shard_map/all_to_all | solution.py:34
  363.0 2.0 maximum_bitcast_fusion
  367.7 15.6 %all-to-all-done.5 = bf16[64,48,128]{2,1,0:T(8,128)(2,1)} async-done(((bf16[64,48,128]{2,1,0:T(8,128)(2,1)}), bf16[64,48,128]{2,1,0:T(8,128)(2,1)}, u32[]{:S(2)}, u32[]{:S(2)}) %all-to-all-start.5) | async-done | bytes 786464 | tf_op jit(solution)/shard_map/all_to_all | solution.py:34
  (110 shorter events, 32.0 us)
Async XLA Ops:
  7.2 72.3 %copy-start = (bf16[128,1]{0,1:T(2,128)(2,1)S(1)}, bf16[128,1]{0,1:T(2,128)(2,1)}, u32[]{:S(2)}) copy-start(bf16[128,1]{0,1:T(2,128)(2,1)} %param.10) | copy-start | bytes 772
  7.2 149.9 %all-gather.9.cloned.1.call-start = ((), (), s32[]{:S(2)}) async-start(), calls=%async_computation.12 | async-start | bytes 3932160 | tf_op jit(solution)/shard_map/all_gather | solution.py:49
  9.6 39.1 %copy-start.18 = (bf16[128,4096]{1,0:T(8,128)(2,1)S(1)}, bf16[128,4096]{1,0:T(8,128)(2,1)}, u32[]{:S(2)}) copy-start(bf16[128,4096]{1,0:T(8,128)(2,1)} %param.7) | copy-start | bytes 3145732
  48.7 114.6 %all-gather.11.cloned.1.call-start = ((), (), s32[]{:S(2)}) async-start(), calls=%async_computation.13 | async-start | bytes 3932160 | tf_op jit(solution)/shard_map/all_gather | solution.py:49
  49.1 37.2 %copy-start.19 = (bf16[128,4096]{1,0:T(8,128)(2,1)S(1)}, bf16[128,4096]{1,0:T(8,128)(2,1)}, u32[]{:S(2)}) copy-start(bf16[128,4096]{1,0:T(8,128)(2,1)} %param.8) | copy-start | bytes 3145732
  80.4 15.2 %all-to-all-start.1 = ((bf16[64,1,3]{2,1,0:T(2,128)(2,1)}), bf16[64,1,3]{2,1,0:T(2,128)(2,1)S(1)}, u32[]{:S(2)}, u32[]{:S(2)}) async-start(bf16[64,1,3]{2,1,0:T(2,128)(2,1)} %all_to_all.40), calls=%async_computation.1 | async-start | bytes 65536 | tf_op jit(solution)/shard_map/all_to_all | solution.py:46
  95.7 27.9 %all-to-all-start = ((bf16[64,48,128]{2,1,0:T(8,128)(2,1)}), bf16[64,48,128]{2,1,0:T(8,128)(2,1)S(1)}, u32[]{:S(2)}, u32[]{:S(2)}) async-start(bf16[64,48,128]{2,1,0:T(8,128)(2,1)} %reshape.105), calls=%async_computation | async-start | bytes 1572864 | tf_op jit(solution)/shard_map/all_to_all | solution.py:34
  100.4 77.8 %all-gather.5.cloned.1.call-start = ((), (), s32[]{:S(2)}) async-start(), calls=%async_computation.10 | async-start | bytes 4177920 | tf_op jit(solution)/shard_map/all_gather | solution.py:58
  125.0 32.1 %copy-start.12 = (bf16[1,4096,192]{1,2,0:T(8,128)(2,1)S(1)}, bf16[1,4096,192]{1,2,0:T(8,128)(2,1)}, u32[]{:S(2)}) copy-start(bf16[1,4096,192]{1,2,0:T(8,128)(2,1)} %param.11) | copy-start | bytes 4718596
  125.0 97.7 %all-gather.7.cloned.1.call-start = ((), (), s32[]{:S(2)}) async-start(), calls=%async_computation.11 | async-start | bytes 3932160 | tf_op jit(solution)/shard_map/all_gather | solution.py:58
  156.8 4.4 %copy-start.14 = (bf16[1,4096,192]{1,2,0:T(8,128)(2,1)S(1)}, bf16[1,4096,192]{1,2,0:T(8,128)(2,1)}, u32[]{:S(2)}) copy-start(bf16[1,4096,192]{1,2,0:T(8,128)(2,1)} %param.12) | copy-start | bytes 4718596
  156.9 118.4 %reduce-scatter.3.cloned.1.call-start = ((), (), s32[]{:S(2)}) async-start(), calls=%async_computation.14 | async-start | bytes 4177920 | tf_op jit(solution)/shard_map/reduce_scatter | solution.py:116
  157.1 4.1 %copy-start.3 = (bf16[768,2048]{1,0:T(8,128)(2,1)S(1)}, bf16[768,2048]{1,0:T(8,128)(2,1)}, u32[]{:S(2)}) copy-start(bf16[768,2048]{1,0:T(8,128)(2,1)} %all-gather.9.cloned.1.call-done) | copy-start | bytes 9437188
  163.3 4.4 %copy-start.2 = (bf16[768,2048]{1,0:T(8,128)(2,1)S(1)}, bf16[768,2048]{1,0:T(8,128)(2,1)}, u32[]{:S(2)}) copy-start(bf16[768,2048]{1,0:T(8,128)(2,1)} %all-gather.11.cloned.1.call-done) | copy-start | bytes 9437188
  163.3 4.4 %copy-start.15 = (bf16[1,4096,192]{1,2,0:T(8,128)(2,1)S(1)}, bf16[1,4096,192]{1,2,0:T(8,128)(2,1)}, u32[]{:S(2)}) copy-start(bf16[1,4096,192]{1,2,0:T(8,128)(2,1)} %param.12) | copy-start | bytes 4718596
  163.3 4.4 %copy-start.25 = (f32[768,192]{0,1:T(8,128)S(1)}, f32[768,192]{0,1:T(8,128)}, u32[]{:S(2)}) copy-start(f32[768,192]{0,1:T(8,128)} %fusion.23) | copy-start | bytes 1769476
  222.7 4.8 %copy-start.13 = (bf16[1,4096,192]{1,2,0:T(8,128)(2,1)S(1)}, bf16[1,4096,192]{1,2,0:T(8,128)(2,1)}, u32[]{:S(2)}) copy-start(bf16[1,4096,192]{1,2,0:T(8,128)(2,1)} %param.11) | copy-start | bytes 4718596
  232.3 85.9 %reduce-scatter.5.cloned.1.call-start = ((), (), s32[]{:S(2)}) async-start(), calls=%async_computation.15 | async-start | bytes 3932160 | tf_op jit(solution)/shard_map/reduce_scatter | solution.py:116
  232.4 2.3 copy-start.6
  232.4 2.3 copy-start.17
  276.9 43.5 %all-to-all-start.7 = ((bf16[64,1,3]{2,1,0:T(2,128)(2,1)}), bf16[64,1,3]{2,1,0:T(2,128)(2,1)S(1)}, u32[]{:S(2)}, u32[]{:S(2)}) async-start(bf16[64,1,3]{2,1,0:T(2,128)(2,1)} %all_to_all.41), calls=%async_computation.9 | async-start | bytes 65536 | tf_op jit(solution)/shard_map/all_to_all | solution.py:119
  320.4 33.9 %all-to-all-start.6 = ((bf16[64,48,128]{2,1,0:T(8,128)(2,1)}), bf16[64,48,128]{2,1,0:T(8,128)(2,1)}, u32[]{:S(2)}, u32[]{:S(2)}) async-start(bf16[64,48,128]{2,1,0:T(8,128)(2,1)} %reshape.116), calls=%async_computation.8 | async-start | bytes 1572864 | tf_op jit(solution)/shard_map/all_to_all | solution.py:34
  331.3 3.7 copy-start.4
  331.4 3.7 copy-start.7
  336.8 2.2 copy-start.26
  338.5 2.3 copy-start.23
  342.6 17.8 %copy-start.8 = (bf16[768,192]{0,1:T(8,128)(2,1)S(1)}, bf16[768,192]{0,1:T(8,128)(2,1)}, u32[]{:S(2)}) copy-start(bf16[768,192]{0,1:T(8,128)(2,1)} %copy-done.5) | copy-start | bytes 884740
  354.3 29.0 %all-to-all-start.5 = ((bf16[64,48,128]{2,1,0:T(8,128)(2,1)}), bf16[64,48,128]{2,1,0:T(8,128)(2,1)}, u32[]{:S(2)}, u32[]{:S(2)}) async-start(bf16[64,48,128]{2,1,0:T(8,128)(2,1)} %reshape.114), calls=%async_computation.6 | async-start | bytes 1572864 | tf_op jit(solution)/shard_map/all_to_all | solution.py:34
  360.4 2.6 copy-start.9
  360.4 2.6 copy-start.10
  360.4 2.6 copy-start.11
  365.9 20.2 %copy-start.1 = (bf16[128,1]{0,1:T(2,128)(2,1)S(1)}, bf16[128,1]{0,1:T(2,128)(2,1)}, u32[]{:S(2)}) copy-start(bf16[128,1]{0,1:T(2,128)(2,1)} %param.10) | copy-start | bytes 772
  (6 other events, 9.0 us)
Sparse Core Ops, SparseCore 0:
  48.8 38.3 all-gather.8
  89.6 42.2 all-gather.10
  134.3 43.8 all-gather.4
  180.4 42.2 all-gather.6
  232.5 42.7 reduce-scatter.2
  277.6 40.5 reduce-scatter.4
where the time goes:
time: 394 us; the launch traced here: 393 us
  waiting for transfers between devices  171 us (43%)
  blocking collectives  93.3 us (24%)
  matrix products  45.1 us (11%)
  starting transfers between devices  38.8 us (10%)
  local copies, waits for them, and re-layouts  19.2 us (5%)
  between operations  14.5 us (4%)
  other arithmetic  11 us (3%)
    all_to_all x3, blocking collectives, to_expert(): lax.all_to_all(shaped, 'expert', 0, 0, tiled=True)  93.3 us
    reduce_scatter x2, waiting for transfers between devices, body(): lax.psum_scatter(part.astype(jnp.bfloat16), 'dp', scatter_dimension=0, ti...  68.4 us
    all_gather x2, waiting for transfers between devices, body(): gathered = lax.all_gather(recv, 'dp', axis=0, tiled=True)  47.9 us
    all_to_all x3, waiting for transfers between devices, to_expert(): lax.all_to_all(shaped, 'expert', 0, 0, tiled=True)  46.9 us
    all_to_all x3, starting transfers between devices, to_expert(): lax.all_to_all(shaped, 'expert', 0, 0, tiled=True)  21.7 us
    all_to_all x1, starting transfers between devices, body(): lax.all_to_all(own_scores, 'expert', 0, 0, tiled=True).reshape(slot_total)  10.8 us
    dot_general x2, matrix products, body(): lax.dot_general(rows_dy[c], down_w[:, c * piece:(c + 1) * piece], contrac...  8.91 us
    dot_general x2, matrix products, body(): jnp.dot(rows_in[c], gate_w[c * piece:(c + 1) * piece], preferred_element_...  8.5 us
  transfers between devices with their start and end apart: 11, of which 8 were waited for; matrix products, arithmetic and copies ran while one was open for 14% of the time, Pallas kernels for 0%

commit v1 on v0

--- a/solution.py
+++ b/solution.py
@@ -55,7 +55,9 @@
             recv = jnp.concatenate(
                 [recv, jnp.broadcast_to(recv_prob[:, None], (slot_total, LANES))], axis=1
             )
-        gathered = lax.all_gather(recv, "dp", axis=0, tiled=True)
+        gathered = jnp.concatenate(
+            lax.all_to_all(jnp.stack([recv] * lax.axis_size("dp")), "dp", 0, 0), axis=0
+        )
         if c == 0:
             rows_prob = gathered[:, piece]
             gathered = gathered[:, :piece]

time: 394 us -> 426 us (1.081)
  waiting for transfers between devices: 171 us -> 234 us
  blocking collectives: 93.3 us -> 35.9 us
  starting transfers between devices: 38.8 us -> 59.2 us
  local copies, waits for them, and re-layouts: 19.2 us -> 27.8 us
    all_to_all x0 -> x2, waiting for transfers between devices: none -> 71.3 us  [body(): lax.all_to_all(jnp.stack([recv] * lax.axis_size('dp')), 'dp', 0, 0)]
    all_to_all x3 -> x1, blocking collectives: 93.3 us -> 35.9 us  [to_expert(): lax.all_to_all(shaped, 'expert', 0, 0, tiled=True)]
    all_gather x2 -> x0, waiting for transfers between devices: 47.9 us -> none  [body(): gathered = lax.all_gather(recv, 'dp', axis=0, tiled=True)]
    all_to_all x3 -> x5, waiting for transfers between devices: 46.9 us -> 86.7 us  [to_expert(): lax.all_to_all(shaped, 'expert', 0, 0, tiled=True)]
    all_to_all x3 -> x5, starting transfers between devices: 21.7 us -> 33.5 us  [to_expert(): lax.all_to_all(shaped, 'expert', 0, 0, tiled=True)]
    all_to_all x0 -> x2, starting transfers between devices: none -> 8.68 us  [body(): lax.all_to_all(jnp.stack([recv] * lax.axis_size('dp')), 'dp', 0, 0)]
    another operation x0 -> x3, local copies, waits for them, and re-layouts: none -> 7.83 us  [body(): jnp.stack([recv] * lax.axis_size('dp'))]
  transfers between devices with their start and end apart: 11 -> 13, of which waited for: 8 -> 10; matrix products, arithmetic and copies ran while one was open for 14% -> 14% of each run, Pallas kernels for 0% -> 0%
where the time goes in v1:
time: 426 us; the launch traced here: 425 us
  waiting for transfers between devices  234 us (55%)
  starting transfers between devices  59.2 us (14%)
  matrix products  44.1 us (10%)
  blocking collectives  35.9 us (8%)
  local copies, waits for them, and re-layouts  27.8 us (7%)
  between operations  14.2 us (3%)
  other arithmetic  9.17 us (2%)
    all_to_all x5, waiting for transfers between devices, to_expert(): lax.all_to_all(shaped, 'expert', 0, 0, tiled=True)  86.7 us
    all_to_all x2, waiting for transfers between devices, body(): lax.all_to_all(jnp.stack([recv] * lax.axis_size('dp')), 'dp', 0, 0)  71.3 us
    reduce_scatter x2, waiting for transfers between devices, body(): lax.psum_scatter(part.astype(jnp.bfloat16), 'dp', scatter_dimension=0, ti...  68.5 us
    all_to_all x1, blocking collectives, to_expert(): lax.all_to_all(shaped, 'expert', 0, 0, tiled=True)  35.9 us
    all_to_all x5, starting transfers between devices, to_expert(): lax.all_to_all(shaped, 'expert', 0, 0, tiled=True)  33.5 us
    all_to_all x1, starting transfers between devices, body(): lax.all_to_all(own_scores, 'expert', 0, 0, tiled=True).reshape(slot_total)  10.7 us
    reshape x6, local copies, waits for them, and re-layouts, to_expert(): shaped = rows.reshape(expert_count, per_peer, LANES)  8.77 us
    all_to_all x2, starting transfers between devices, body(): lax.all_to_all(jnp.stack([recv] * lax.axis_size('dp')), 'dp', 0, 0)  8.68 us
  transfers between devices with their start and end apart: 13, of which 10 were waited for; matrix products, arithmetic and copies ran while one was open for 14% of the time, Pallas kernels for 0%

profile of v1, /device:TPU:1, one launch (start us, length us, event | category | flops | bytes accessed | tf_op | source)
XLA Modules:
  0.0 424.7 jit_solution(16709124078026857130)
XLA Ops:
  11.4 35.9 %all_to_all.60 = bf16[64,48,128]{2,1,0:T(8,128)(2,1)S(1)} all-to-all(bf16[64,48,128]{2,1,0:T(8,128)(2,1)S(1)} %reshape.118), channel_id=1, replica_groups=mesh['dp'=4,'expert'=64] {'expert'}, dimensions={0} | all-to-all | bytes 1572864 | tf_op jit(solution)/shard_map/all_to_all | solution.py:34
  49.6 5.9 %all-to-all-start.1 = ((bf16[64,1,3]{2,1,0:T(2,128)(2,1)}), bf16[64,1,3]{2,1,0:T(2,128)(2,1)S(1)}, u32[]{:S(2)}, u32[]{:S(2)}) async-start(bf16[64,1,3]{2,1,0:T(2,128)(2,1)} %all_to_all.48), calls=%async_computation.1 | async-start | bytes 65536 | tf_op jit(solution)/shard_map/all_to_all | solution.py:46
  57.1 7.7 %all-to-all-done.1 = bf16[64,1,3]{2,1,0:T(2,128)(2,1)S(1)} async-done(((bf16[64,1,3]{2,1,0:T(2,128)(2,1)}), bf16[64,1,3]{2,1,0:T(2,128)(2,1)S(1)}, u32[]{:S(2)}, u32[]{:S(2)}) %all-to-all-start.1) | async-done | bytes 416 | tf_op jit(solution)/shard_map/all_to_all | solution.py:46
  64.8 4.8 %all-to-all-start.6 = ((bf16[64,48,128]{2,1,0:T(8,128)(2,1)}), bf16[64,48,128]{2,1,0:T(8,128)(2,1)S(1)}, u32[]{:S(2)}, u32[]{:S(2)}) async-start(bf16[64,48,128]{2,1,0:T(8,128)(2,1)} %reshape.120), calls=%async_computation.6 | async-start | bytes 1572864 | tf_op jit(solution)/shard_map/all_to_all | solution.py:34
  72.2 20.5 %all-to-all-done.6 = bf16[64,48,128]{2,1,0:T(8,128)(2,1)S(1)} async-done(((bf16[64,48,128]{2,1,0:T(8,128)(2,1)}), bf16[64,48,128]{2,1,0:T(8,128)(2,1)S(1)}, u32[]{:S(2)}, u32[]{:S(2)}) %all-to-all-start.6) | async-done | bytes 786464 | tf_op jit(solution)/shard_map/all_to_all | solution.py:34
  92.8 5.8 %all-to-all-start = ((bf16[64,48,128]{2,1,0:T(8,128)(2,1)}), bf16[64,48,128]{2,1,0:T(8,128)(2,1)S(1)}, u32[]{:S(2)}, u32[]{:S(2)}) async-start(bf16[64,48,128]{2,1,0:T(8,128)(2,1)} %reshape.112), calls=%async_computation | async-start | bytes 1572864 | tf_op jit(solution)/shard_map/all_to_all | solution.py:34
  100.2 21.4 %all-to-all-done = bf16[64,48,128]{2,1,0:T(8,128)(2,1)S(1)} async-done(((bf16[64,48,128]{2,1,0:T(8,128)(2,1)}), bf16[64,48,128]{2,1,0:T(8,128)(2,1)S(1)}, u32[]{:S(2)}, u32[]{:S(2)}) %all-to-all-start) | async-done | bytes 786464 | tf_op jit(solution)/shard_map/all_to_all | solution.py:34
  121.6 5.9 %all-to-all-start.3 = ((bf16[64,48,128]{2,1,0:T(8,128)(2,1)}), bf16[64,48,128]{2,1,0:T(8,128)(2,1)S(1)}, u32[]{:S(2)}, u32[]{:S(2)}) async-start(bf16[64,48,128]{2,1,0:T(8,128)(2,1)} %reshape.116), calls=%async_computation.3 | async-start | bytes 1572864 | tf_op jit(solution)/shard_map/all_to_all | solution.py:34
  129.6 21.0 %all-to-all-done.3 = bf16[64,48,128]{2,1,0:T(8,128)(2,1)S(1)} async-done(((bf16[64,48,128]{2,1,0:T(8,128)(2,1)}), bf16[64,48,128]{2,1,0:T(8,128)(2,1)S(1)}, u32[]{:S(2)}, u32[]{:S(2)}) %all-to-all-start.3) | async-done | bytes 786464 | tf_op jit(solution)/shard_map/all_to_all | solution.py:34
  152.5 4.0 all-to-all-start.2
  156.5 2.1 stack_reshape.2
  158.7 50.6 %all-to-all-done.2 = bf16[4,192,2176]{2,1,0:T(8,128)(2,1)S(1)} async-done(((bf16[4,192,2176]{2,1,0:T(8,128)(2,1)}), bf16[4,192,2176]{2,1,0:T(8,128)(2,1)S(1)}, u32[]{:S(2)}, u32[]{:S(2)}) %all-to-all-start.2) | async-done | bytes 3342368 | tf_op jit(solution)/shard_map/all_to_all | solution.py:59
  209.3 3.7 stack.5
  213.0 4.7 %all-to-all-start.4 = ((bf16[4,192,2048]{2,1,0:T(8,128)(2,1)}), bf16[4,192,2048]{2,1,0:T(8,128)(2,1)}, u32[]{:S(2)}, u32[]{:S(2)}) async-start(bf16[4,192,2048]{2,1,0:T(8,128)(2,1)} %stack.5), calls=%async_computation.4 | async-start | bytes 6291456 | tf_op jit(solution)/shard_map/all_to_all | solution.py:59
  218.1 3.1 fusion.5
  221.2 4.2 fusion.18
  227.5 4.4 %convolution_add_fusion = f32[768,192]{0,1:T(8,128)} fusion(f32[768,192]{0,1:T(8,128)} %fusion.18, bf16[768,2048]{1,0:T(8,128)(2,1)} %all-gather.5.cloned.1.call-done, bf16[1,4096,192]{1,2,0:T(8,128)(2,1)} %param.11), kind=kOutput, calls=%fused_computation.27 | convolution fusion | flops 604127232 | bytes 5111808 | tf_op jit(solution)/shard_map/dot_general | solution.py:71
  233.9 20.7 %all-to-all-done.4 = bf16[4,192,2048]{2,1,0:T(8,128)(2,1)} async-done(((bf16[4,192,2048]{2,1,0:T(8,128)(2,1)}), bf16[4,192,2048]{2,1,0:T(8,128)(2,1)}, u32[]{:S(2)}, u32[]{:S(2)}) %all-to-all-start.4) | async-done | bytes 3145760 | tf_op jit(solution)/shard_map/all_to_all | solution.py:59
  254.6 4.8 %multiply_reduce_fusion = (bf16[768]{0:T(1024)(128)(2,1)S(1)}, bf16[768,192]{0,1:T(8,128)(2,1)}, bf16[768,192]{0,1:T(8,128)(2,1)S(1)}, bf16[768,192]{0,1:T(8,128)(2,1)S(1)}) fusion(f32[768,192]{0,1:T(8,128)} %convolution_add_fusion.1, f32[768,192]{0,1:T(8,128)} %convolution_add_fusion, f32[768]{0:T(1024)S(1)} %convert_reduce_fusion, f32[768,192]{0,1:T(8,128)} %fusion.5, ...), kind=kOutput, calls=%fused_computation.57 | convolution fusion | flops 606928128 | bytes 6590976 | tf_op jit(solution)/shard_map/dot_general | solution.py:84
  262.1 2.0 pad_maximum_fusion
  264.3 2.3 fusion.13
  266.6 2.7 add_convert_fusion
  269.3 38.0 %reduce-scatter.3.cloned.1.call-done = bf16[192,2176]{1,0:T(8,128)(2,1)} async-done(((bf16[768,2176]{1,0:T(8,128)(2,1)}), bf16[192,2176]{1,0:T(8,128)(2,1)}) %reduce-scatter.3.cloned.1.call-update) | async-done | bytes 835600 | tf_op jit(solution)/shard_map/reduce_scatter | solution.py:118
  309.0 10.7 %all-to-all-start.9 = ((bf16[64,1,3]{2,1,0:T(2,128)(2,1)}), bf16[64,1,3]{2,1,0:T(2,128)(2,1)S(1)}, u32[]{:S(2)}, u32[]{:S(2)}) async-start(bf16[64,1,3]{2,1,0:T(2,128)(2,1)} %all_to_all.49), calls=%async_computation.11 | async-start | bytes 65536 | tf_op jit(solution)/shard_map/all_to_all | solution.py:121
  319.7 30.5 %reduce-scatter.5.cloned.1.call-done = bf16[192,2048]{1,0:T(8,128)(2,1)} async-done(((bf16[768,2048]{1,0:T(8,128)(2,1)}), bf16[192,2048]{1,0:T(8,128)(2,1)}) %reduce-scatter.5.cloned.1.call-update) | async-done | bytes 786448 | tf_op jit(solution)/shard_map/reduce_scatter | solution.py:118
  350.2 2.2 reshape.124
  352.4 10.9 %all-to-all-start.8 = ((bf16[64,48,128]{2,1,0:T(8,128)(2,1)}), bf16[64,48,128]{2,1,0:T(8,128)(2,1)}, u32[]{:S(2)}, u32[]{:S(2)}) async-start(bf16[64,48,128]{2,1,0:T(8,128)(2,1)} %reshape.124), calls=%async_computation.10 | async-start | bytes 1572864 | tf_op jit(solution)/shard_map/all_to_all | solution.py:34
  368.9 3.8 fusion.8
  375.5 2.5 reshape.122
  378.1 8.2 %all-to-all-done.8 = bf16[64,48,128]{2,1,0:T(8,128)(2,1)} async-done(((bf16[64,48,128]{2,1,0:T(8,128)(2,1)}), bf16[64,48,128]{2,1,0:T(8,128)(2,1)}, u32[]{:S(2)}, u32[]{:S(2)}) %all-to-all-start.8) | async-done | bytes 786464 | tf_op jit(solution)/shard_map/all_to_all | solution.py:34
  386.3 6.1 %all-to-all-start.7 = ((bf16[64,48,128]{2,1,0:T(8,128)(2,1)}), bf16[64,48,128]{2,1,0:T(8,128)(2,1)}, u32[]{:S(2)}, u32[]{:S(2)}) async-start(bf16[64,48,128]{2,1,0:T(8,128)(2,1)} %reshape.122), calls=%async_computation.8 | async-start | bytes 1572864 | tf_op jit(solution)/shard_map/all_to_all | solution.py:34
  399.8 15.6 %all-to-all-done.7 = bf16[64,48,128]{2,1,0:T(8,128)(2,1)} async-done(((bf16[64,48,128]{2,1,0:T(8,128)(2,1)}), bf16[64,48,128]{2,1,0:T(8,128)(2,1)}, u32[]{:S(2)}, u32[]{:S(2)}) %all-to-all-start.7) | async-done | bytes 786464 | tf_op jit(solution)/shard_map/all_to_all | solution.py:34
  (114 shorter events, 43.5 us)
Async XLA Ops:
  7.2 41.4 %copy-start = (bf16[128,1]{0,1:T(2,128)(2,1)S(1)}, bf16[128,1]{0,1:T(2,128)(2,1)}, u32[]{:S(2)}) copy-start(bf16[128,1]{0,1:T(2,128)(2,1)} %param.10) | copy-start | bytes 772
  7.2 214.0 %all-gather.3.cloned.1.call-start = ((), (), s32[]{:S(2)}) async-start(), calls=%async_computation.12 | async-start | bytes 3932160 | tf_op jit(solution)/shard_map/all_gather | solution.py:49
  11.0 44.5 %copy-start.21 = (bf16[128,4096]{1,0:T(8,128)(2,1)S(1)}, bf16[128,4096]{1,0:T(8,128)(2,1)}, u32[]{:S(2)}) copy-start(bf16[128,4096]{1,0:T(8,128)(2,1)} %param.7) | copy-start | bytes 3145732
  49.6 15.2 %all-to-all-start.1 = ((bf16[64,1,3]{2,1,0:T(2,128)(2,1)}), bf16[64,1,3]{2,1,0:T(2,128)(2,1)S(1)}, u32[]{:S(2)}, u32[]{:S(2)}) async-start(bf16[64,1,3]{2,1,0:T(2,128)(2,1)} %all_to_all.48), calls=%async_computation.1 | async-start | bytes 65536 | tf_op jit(solution)/shard_map/all_to_all | solution.py:46
  57.1 41.5 %copy-start.22 = (bf16[128,4096]{1,0:T(8,128)(2,1)S(1)}, bf16[128,4096]{1,0:T(8,128)(2,1)}, u32[]{:S(2)}) copy-start(bf16[128,4096]{1,0:T(8,128)(2,1)} %param.8) | copy-start | bytes 3145732
  64.8 27.9 %all-to-all-start.6 = ((bf16[64,48,128]{2,1,0:T(8,128)(2,1)}), bf16[64,48,128]{2,1,0:T(8,128)(2,1)S(1)}, u32[]{:S(2)}, u32[]{:S(2)}) async-start(bf16[64,48,128]{2,1,0:T(8,128)(2,1)} %reshape.120), calls=%async_computation.6 | async-start | bytes 1572864 | tf_op jit(solution)/shard_map/all_to_all | solution.py:34
  92.8 28.9 %all-to-all-start = ((bf16[64,48,128]{2,1,0:T(8,128)(2,1)}), bf16[64,48,128]{2,1,0:T(8,128)(2,1)S(1)}, u32[]{:S(2)}, u32[]{:S(2)}) async-start(bf16[64,48,128]{2,1,0:T(8,128)(2,1)} %reshape.112), calls=%async_computation | async-start | bytes 1572864 | tf_op jit(solution)/shard_map/all_to_all | solution.py:34
  121.6 28.9 %all-to-all-start.3 = ((bf16[64,48,128]{2,1,0:T(8,128)(2,1)}), bf16[64,48,128]{2,1,0:T(8,128)(2,1)S(1)}, u32[]{:S(2)}, u32[]{:S(2)}) async-start(bf16[64,48,128]{2,1,0:T(8,128)(2,1)} %reshape.116), calls=%async_computation.3 | async-start | bytes 1572864 | tf_op jit(solution)/shard_map/all_to_all | solution.py:34
  127.5 99.9 %all-gather.5.cloned.1.call-start = ((), (), s32[]{:S(2)}) async-start(), calls=%async_computation.13 | async-start | bytes 3932160 | tf_op jit(solution)/shard_map/all_gather | solution.py:49
  152.5 56.8 %all-to-all-start.2 = ((bf16[4,192,2176]{2,1,0:T(8,128)(2,1)}), bf16[4,192,2176]{2,1,0:T(8,128)(2,1)S(1)}, u32[]{:S(2)}, u32[]{:S(2)}) async-start(bf16[4,192,2176]{2,1,0:T(8,128)(2,1)} %stack.4), calls=%async_computation.2 | async-start | bytes 6684672 | tf_op jit(solution)/shard_map/all_to_all | solution.py:59
  209.3 8.8 %copy-start.10 = (bf16[4,192,2176]{2,1,0:T(8,128)(2,1)}, bf16[4,192,2176]{2,1,0:T(8,128)(2,1)S(1)}, u32[]{:S(2)}) copy-start(bf16[4,192,2176]{2,1,0:T(8,128)(2,1)S(1)} %all-to-all-done.2) | copy-start | bytes 10027012
  213.0 41.6 %all-to-all-start.4 = ((bf16[4,192,2048]{2,1,0:T(8,128)(2,1)}), bf16[4,192,2048]{2,1,0:T(8,128)(2,1)}, u32[]{:S(2)}, u32[]{:S(2)}) async-start(bf16[4,192,2048]{2,1,0:T(8,128)(2,1)} %stack.5), calls=%async_computation.4 | async-start | bytes 6291456 | tf_op jit(solution)/shard_map/all_to_all | solution.py:59
  217.7 89.6 %reduce-scatter.3.cloned.1.call-start = ((), (), s32[]{:S(2)}) async-start(), calls=%async_computation.14 | async-start | bytes 4177920 | tf_op jit(solution)/shard_map/reduce_scatter | solution.py:118
  221.2 4.2 copy-start.2
  221.2 4.2 copy-start.17
  227.5 4.4 %copy-start.3 = (bf16[768,2048]{1,0:T(8,128)(2,1)S(1)}, bf16[768,2048]{1,0:T(8,128)(2,1)}, u32[]{:S(2)}) copy-start(bf16[768,2048]{1,0:T(8,128)(2,1)} %all-gather.5.cloned.1.call-done) | copy-start | bytes 9437188
  227.5 4.4 %copy-start.18 = (bf16[1,4096,192]{1,2,0:T(8,128)(2,1)S(1)}, bf16[1,4096,192]{1,2,0:T(8,128)(2,1)}, u32[]{:S(2)}) copy-start(bf16[1,4096,192]{1,2,0:T(8,128)(2,1)} %param.12) | copy-start | bytes 4718596
  227.5 4.4 %copy-start.26 = (f32[768,192]{0,1:T(8,128)S(1)}, f32[768,192]{0,1:T(8,128)}, u32[]{:S(2)}) copy-start(f32[768,192]{0,1:T(8,128)} %fusion.23) | copy-start | bytes 1769476
  254.6 4.8 %copy-start.16 = (bf16[1,4096,192]{1,2,0:T(8,128)(2,1)S(1)}, bf16[1,4096,192]{1,2,0:T(8,128)(2,1)}, u32[]{:S(2)}) copy-start(bf16[1,4096,192]{1,2,0:T(8,128)(2,1)} %param.11) | copy-start | bytes 4718596
  264.2 86.1 %reduce-scatter.5.cloned.1.call-start = ((), (), s32[]{:S(2)}) async-start(), calls=%async_computation.15 | async-start | bytes 3932160 | tf_op jit(solution)/shard_map/reduce_scatter | solution.py:118
  264.2 2.3 copy-start.7
  264.2 2.3 copy-start.20
  309.0 43.5 %all-to-all-start.9 = ((bf16[64,1,3]{2,1,0:T(2,128)(2,1)}), bf16[64,1,3]{2,1,0:T(2,128)(2,1)S(1)}, u32[]{:S(2)}, u32[]{:S(2)}) async-start(bf16[64,1,3]{2,1,0:T(2,128)(2,1)} %all_to_all.49), calls=%async_computation.11 | async-start | bytes 65536 | tf_op jit(solution)/shard_map/all_to_all | solution.py:121
  352.4 33.9 %all-to-all-start.8 = ((bf16[64,48,128]{2,1,0:T(8,128)(2,1)}), bf16[64,48,128]{2,1,0:T(8,128)(2,1)}, u32[]{:S(2)}, u32[]{:S(2)}) async-start(bf16[64,48,128]{2,1,0:T(8,128)(2,1)} %reshape.124), calls=%async_computation.10 | async-start | bytes 1572864 | tf_op jit(solution)/shard_map/all_to_all | solution.py:34
  368.9 3.8 copy-start.11
  374.6 17.8 %copy-start.5 = (bf16[768,2048]{1,0:T(8,128)(2,1)S(1)}, bf16[768,2048]{1,0:T(8,128)(2,1)}, u32[]{:S(2)}) copy-start(bf16[768,2048]{1,0:T(8,128)(2,1)} %all-gather.5.cloned.1.call-done) | copy-start | bytes 9437188
  374.6 17.8 %copy-start.9 = (bf16[768,192]{0,1:T(8,128)(2,1)S(1)}, bf16[768,192]{0,1:T(8,128)(2,1)}, u32[]{:S(2)}) copy-start(bf16[768,192]{0,1:T(8,128)(2,1)} %copy-done.6) | copy-start | bytes 884740
  386.3 29.0 %all-to-all-start.7 = ((bf16[64,48,128]{2,1,0:T(8,128)(2,1)}), bf16[64,48,128]{2,1,0:T(8,128)(2,1)}, u32[]{:S(2)}, u32[]{:S(2)}) async-start(bf16[64,48,128]{2,1,0:T(8,128)(2,1)} %reshape.122), calls=%async_computation.8 | async-start | bytes 1572864 | tf_op jit(solution)/shard_map/all_to_all | solution.py:34
  392.4 2.6 copy-start.12
  392.4 2.6 copy-start.13
  392.4 2.6 copy-start.14
  398.0 20.2 %copy-start.1 = (bf16[128,1]{0,1:T(2,128)(2,1)S(1)}, bf16[128,1]{0,1:T(2,128)(2,1)}, u32[]{:S(2)}) copy-start(bf16[128,1]{0,1:T(2,128)(2,1)} %param.10) | copy-start | bytes 772
  (9 other events, 14.4 us)
Sparse Core Ops, SparseCore 0:
  48.7 38.3 all-gather.2
  130.7 54.8 all-gather.4
  264.3 42.9 reduce-scatter.2
  309.7 40.5 reduce-scatter.4
